TPU v7x, 256 devices: a whole 4x4x8 slice. The times are simulated.
256 devices in a mesh: grp: 32 (over x, z), shard: 8 (over y, core).
Axes of the slice: x: 4, y: 4, z: 8, core: 2. Of those that a mesh axis runs over, the one named last changes fastest.
Arguments:
- layer_inputs: bfloat16 [131072, 1600], P(('grp', 'shard')), may hold values from -6 to 6
- cotangents: bfloat16 [131072, 1600], P(('grp', 'shard')), may hold values from -0.25 to 0.25
- weight: bfloat16 [1600, 1600], P('shard'), may hold values from -0.15625 to 0.15625
- error_state: float32 [32, 1600, 1600], P('grp', 'shard'), may hold values from -6 to 6
- momentum: float32 [1600, 1600], P('shard'), may hold values from -0.75 to 0.75
- bias_momentum: float32 [1600], replicated, may hold values from -6 to 6
- start_basis: float32 [1600, 32], replicated, may hold values from -6 to 6
- next_inputs: bfloat16 [131072, 1600], P(('grp', 'shard')), may hold values from -6 to 6
Outputs:
- next_outputs: bfloat16 [131072, 1600], P(('grp', 'shard'))
- new_error: float32 [32, 1600, 1600], P('grp', 'shard')
- new_momentum: float32 [1600, 1600], P('shard')
- new_bias_momentum: float32 [1600], replicated
All inputs are finite; a program needn't handle non-finite values.
Results may differ from a plain program's by a relative error of at most 0.015.
Values may be sent and summed in bfloat16 or wider, within the bound.
No kernel may reach another device: no remote copies, remote signals or barrier semaphores. Data moves between devices by JAX's collectives and lax.ppermute only.
A program may use at most 128 MiB of HBM per device.

v0:
```python
import jax
import jax.numpy as jnp
from jax import lax
from jax.sharding import PartitionSpec as P

momentum_decay = 0.9
learn_rate = 0.1


def shards(
    layer_inputs, cotangents, weight, error_state, momentum, bias_momentum, start_basis, next_inputs
):
    highest = lax.Precision.HIGHEST
    group_count = lax.axis_size("grp")
    rank = start_basis.shape[1]
    gradient = lax.psum_scatter(
        lax.dot_general(
            layer_inputs, cotangents, (((0,), (0,)), ((), ())), preferred_element_type=jnp.float32
        ).astype(jnp.bfloat16),
        "shard",
        scatter_dimension=0,
        tiled=True,
    ).astype(jnp.float32)
    column_sums = jnp.sum(cotangents, axis=0, dtype=jnp.float32)
    corrected = gradient + error_state[0]
    summed = lax.psum(jnp.concatenate([corrected, column_sums[None, :]], axis=0), "grp")
    total = summed[:-1]
    grp_sums = summed[-1]
    basis = start_basis
    ortho = start_basis
    for round_index in range(2):
        factor = jnp.dot(total, basis, precision=highest)
        gram_part = jnp.dot(factor.T, factor, precision=highest)
        if round_index == 0:
            packed = lax.psum(jnp.concatenate([gram_part.reshape(-1), grp_sums]), "shard")
            gram = packed[: rank * rank].reshape(rank, rank)
            all_sums = packed[rank * rank :]
        else:
            gram = lax.psum(gram_part, "shard")
        lower_factor = jnp.linalg.cholesky(gram)
        ortho = jax.scipy.linalg.solve_triangular(lower_factor, factor.T, lower=True).T
        partial_basis = lax.dot_general(total, ortho, (((0,), (0,)), ((), ())), precision=highest)
        basis = lax.psum(partial_basis, "shard") / group_count
    approx = jnp.dot(ortho, basis.T, precision=highest)
    new_error = (corrected - approx)[None, :, :]
    new_momentum = momentum_decay * momentum + approx
    new_bias_momentum = momentum_decay * bias_momentum + all_sums / group_count
    new_weight = (weight.astype(jnp.float32) - learn_rate * new_momentum).astype(jnp.bfloat16)
    projected = jnp.dot(
        next_inputs,
        lax.all_gather(new_weight, "shard", axis=0, tiled=True),
        preferred_element_type=jnp.float32,
    )
    return (projected.astype(jnp.bfloat16), new_error, new_momentum, new_bias_momentum)


def solution(mesh):
    placed = (
        P(("grp", "shard"), None),
        P(("grp", "shard"), None),
        P("shard", None),
        P("grp", "shard", None),
        P("shard", None),
        P(),
        P(),
        P(("grp", "shard"), None),
    )
    return jax.shard_map(
        shards,
        mesh=mesh,
        in_specs=placed,
        out_specs=(P(("grp", "shard"), None), P("grp", "shard", None), P("shard", None), P()),
        check_vma=False,
    )
```

profile of v0, /device:TPU:1, one launch (start us, length us, event | category | flops | bytes accessed | tf_op | source)
XLA Modules:
  0.0 473.4 jit_solution(3598170805652788617)
XLA Ops:
  7.2 1.4 copy-done
  8.6 6.3 %convolution_convert_fusion = bf16[1600,1600]{1,0:T(8,128)(2,1)} fusion(bf16[512,1600]{0,1:T(8,128)(2,1)S(1)} %copy-done, bf16[512,1600]{0,1:T(8,128)(2,1)} %param.12), kind=kOutput, calls=%fused_computation | convolution fusion | flops 2624000000 | bytes 8396800 | tf_op jit(solution)/shard_map/dot_general | solution.py:17
  15.0 1.4 copy-done.3
  16.7 48.7 %reduce-scatter.4.cloned.1.call-done = bf16[200,1600]{1,0:T(8,128)(2,1)} async-done(((bf16[1600,1600]{1,0:T(8,128)(2,1)}), bf16[200,1600]{1,0:T(8,128)(2,1)}) %reduce-scatter.4.cloned.1.call-update) | async-done | bytes 640016
  65.4 1.6 bitcast_add_fusion
  67.0 1.1 copy-done.2
  68.1 1.2 pad_maximum_fusion
  69.3 149.4 %all-reduce.5.cloned.1.call-done = f32[201,1600]{1,0:T(8,128)} async-done(((f32[201,1600]{1,0:T(8,128)}), f32[201,1600]{1,0:T(8,128)}) %all-reduce.5.cloned.1.call-update) | async-done | bytes 1286416 | tf_op jit(solution)/shard_map/psum | solution.py:26
  218.7 2.8 fusion.7
  221.8 25.7 %psum.36 = f32[2624]{0:T(1024)S(1)} all-reduce(f32[2624]{0:T(1024)S(1)} %pad_maximum_fusion.1), channel_id=1, replica_groups=mesh['grp'=32,'shard'=8] {'shard'}, use_global_device_ids=true, to_apply=%region_3.0 | all-reduce | flops 2624 | bytes 20992 | tf_op jit(solution)/shard_map/psum | solution.py:35
  247.7 2.9 cholesky.44
  251.3 0.7 fusion.18
  251.9 2.4 custom-call.6
  254.6 1.7 fusion.5
  256.4 60.6 %all-reduce.7.cloned.1.call-done = f32[1600,32]{0,1:T(8,128)} async-done(((f32[1600,32]{0,1:T(8,128)}), f32[1600,32]{0,1:T(8,128)}) %all-reduce.7.cloned.1.call-update) | async-done | bytes 204816 | tf_op jit(solution)/shard_map/psum | solution.py:43
  317.0 2.3 fusion.3
  319.4 21.9 %psum.38 = f32[32,32]{0,1:T(8,128)S(1)} all-reduce(f32[32,32]{0,1:T(8,128)S(1)} %fusion.32), channel_id=1, replica_groups=mesh['grp'=32,'shard'=8] {'shard'}, use_global_device_ids=true, to_apply=%region_7.10 | all-reduce | flops 1024 | bytes 8192 | tf_op jit(solution)/shard_map/psum | solution.py:39
  341.4 2.9 cholesky.55
  345.7 2.4 custom-call.7
  348.3 1.7 fusion.1
  350.1 64.9 %all-reduce.9.cloned.1.call-done = f32[1600,32]{0,1:T(8,128)} async-done(((f32[1600,32]{0,1:T(8,128)}), f32[1600,32]{0,1:T(8,128)}) %all-reduce.9.cloned.1.call-update) | async-done | bytes 204816 | tf_op jit(solution)/shard_map/psum | solution.py:43
  415.0 5.2 %subtract_convert_fusion = (bf16[200,1600]{1,0:T(8,128)(2,1)}, f32[200,1600]{1,0:T(8,128)}, f32[1,200,1600]{2,1,0:T(8,128)}) fusion(bf16[200,1600]{1,0:T(8,128)(2,1)} %param.13, f32[200,1600]{1,0:T(8,128)} %param.15, f32[200,1600]{1,0:T(8,128)} %copy-done.2, f32[32,200]{1,0:T(8,128)S(1)} %fusion.14, f32[1600,32]{0,1:T(8,128)} %all-reduce.9.cloned.1.call-done), kind=kOutput, calls=%fused_computation.7 | convolution fusion | flops 125171200 | bytes 6630400 | tf_op jit(solution)/shard_map/dot_general | solution.py:44
  420.8 38.7 %all-gather.2.cloned.1.call-done = bf16[1600,1600]{1,0:T(8,128)(2,1)} async-done(((bf16[200,1600]{1,0:T(8,128)(2,1)}), bf16[1600,1600]{1,0:T(8,128)(2,1)}) %all-gather.2.cloned.1.call-update) | async-done | bytes 5120016 | tf_op jit(solution)/shard_map/all_gather | solution.py:51
  459.5 7.4 %fusion = bf16[512,1600]{0,1:T(8,128)(2,1)} fusion(bf16[1600,1600]{1,0:T(8,128)(2,1)} %all-gather.2.cloned.1.call-done, bf16[512,1600]{0,1:T(8,128)(2,1)} %param.18), kind=kOutput, calls=%fused_computation.3 | convolution fusion | flops 2622259200 | bytes 8396800 | tf_op jit(solution)/shard_map/dot_general | solution.py:49
  (40 shorter events, 4.4 us)
Async XLA Ops:
  7.2 1.4 copy-start
  7.2 58.2 %reduce-scatter.4.cloned.1.call-start = ((), (), s32[]{:S(2)}) async-start(), calls=%async_computation.5 | async-start | bytes 5990400
  14.9 1.4 copy-start.3
  14.9 203.7 %all-reduce.5.cloned.1.call-start = ((), (), s32[]{:S(2)}) async-start(), calls=%async_computation.1 | async-start | bytes 2768896 | tf_op jit(solution)/shard_map/psum | solution.py:26
  67.0 1.1 copy-start.2
  68.1 150.6 %copy-start.4 = (f32[1600,32]{0,1:T(8,128)S(1)}, f32[1600,32]{0,1:T(8,128)}, u32[]{:S(2)}) copy-start(f32[1600,32]{0,1:T(8,128)} %param.17) | copy-start | bytes 614404
  69.3 247.7 %all-reduce.7.cloned.1.call-start = ((), (), s32[]{:S(2)}) async-start(), calls=%async_computation.2 | async-start | bytes 425984 | tf_op jit(solution)/shard_map/psum | solution.py:43
  218.7 3.0 copy-start.1
  256.3 158.7 %all-reduce.9.cloned.1.call-start = ((), (), s32[]{:S(2)}) async-start(), calls=%async_computation.3 | async-start | bytes 425984 | tf_op jit(solution)/shard_map/psum | solution.py:43
  350.0 70.2 %copy-start.5 = (f32[1600]{0:T(1024)S(1)}, f32[1600]{0:T(1024)}, u32[]{:S(2)}) copy-start(f32[1600]{0:T(1024)} %param.16) | copy-start | bytes 19204
  350.0 109.5 %all-gather.2.cloned.1.call-start = ((), (), s32[]{:S(2)}) async-start(), calls=%async_computation.4 | async-start | bytes 5990400 | tf_op jit(solution)/shard_map/all_gather | solution.py:51
Sparse Core Ops, SparseCore 0:
  15.1 50.2 reduce-scatter.3
  69.4 149.1 all-reduce.4
  256.4 60.4 all-reduce.6
  350.1 64.7 all-reduce.8
  420.3 39.1 all-gather.1
where the time goes:
time: 474 us; the launch traced here: 473 us
  waiting for transfers between devices  362 us (76%)
  blocking collectives  47.7 us (10%)
  matrix products  28.1 us (6%)
  other arithmetic  17.1 us (4%)
  between operations  13.9 us (3%)
    psum x1, waiting for transfers between devices, shards(): lax.psum(jnp.concatenate([corrected, column_sums[None, :]], axis=0), 'grp')  149 us
    psum x2, waiting for transfers between devices, shards(): basis = lax.psum(partial_basis, 'shard') / group_count  125 us
    unnamed x6, waiting for transfers between devices  48.8 us
    all_gather x1, waiting for transfers between devices, shards(): lax.all_gather(new_weight, 'shard', axis=0, tiled=True)  38.7 us
    psum x1, blocking collectives, shards(): lax.psum(jnp.concatenate([gram_part.reshape(-1), grp_sums]), 'shard')  25.7 us
    psum x1, blocking collectives, shards(): gram = lax.psum(gram_part, 'shard')  21.9 us
  transfers between devices with their start and end apart: 5, of which 5 were waited for; matrix products, arithmetic and copies ran while one was open for 0% of the time, Pallas kernels for 0%

commit v1 on v0

--- a/solution.py
+++ b/solution.py
@@ -5,6 +5,7 @@
 
 momentum_decay = 0.9
 learn_rate = 0.1
+read_clusters_here = lambda array_here, a_name: jnp.sum(lax.all_gather(array_here, a_name), 0)
 
 
 def shards(
@@ -40,7 +41,7 @@
         lower_factor = jnp.linalg.cholesky(gram)
         ortho = jax.scipy.linalg.solve_triangular(lower_factor, factor.T, lower=True).T
         partial_basis = lax.dot_general(total, ortho, (((0,), (0,)), ((), ())), precision=highest)
-        basis = lax.psum(partial_basis, "shard") / group_count
+        basis = read_clusters_here(partial_basis, "shard") / group_count
     approx = jnp.dot(ortho, basis.T, precision=highest)
     new_error = (corrected - approx)[None, :, :]
     new_momentum = momentum_decay * momentum + approx

time: 474 us -> 404 us (0.85)
  waiting for transfers between devices: 362 us -> 291 us
    psum x2 -> x0, waiting for transfers between devices: 125 us -> none  [shards(): basis = lax.psum(partial_basis, 'shard') / group_count]
    all_gather x0 -> x2, waiting for transfers between devices: none -> 54.1 us  [lax.all_gather(array_here, a_name)]
where the time goes in v1:
time: 404 us; the launch traced here: 403 us
  waiting for transfers between devices  291 us (72%)
  blocking collectives  46.8 us (12%)
  matrix products  26.7 us (7%)
  other arithmetic  20.2 us (5%)
  between operations  13.9 us (3%)
  local copies, waits for them, and re-layouts  4.13 us (1%)
    psum x1, waiting for transfers between devices, shards(): lax.psum(jnp.concatenate([corrected, column_sums[None, :]], axis=0), 'grp')  149 us
    all_gather x2, waiting for transfers between devices, lax.all_gather(array_here, a_name)  54.1 us
    unnamed x6, waiting for transfers between devices  48.8 us
    all_gather x1, waiting for transfers between devices, shards(): lax.all_gather(new_weight, 'shard', axis=0, tiled=True)  39.2 us
    psum x1, blocking collectives, shards(): lax.psum(jnp.concatenate([gram_part.reshape(-1), grp_sums]), 'shard')  25.7 us
    psum x1, blocking collectives, shards(): gram = lax.psum(gram_part, 'shard')  21.1 us
  transfers between devices with their start and end apart: 5, of which 5 were waited for; matrix products, arithmetic and copies ran while one was open for 0% of the time, Pallas kernels for 0%

profile of v1, /device:TPU:1, one launch (start us, length us, event | category | flops | bytes accessed | tf_op | source)
XLA Modules:
  0.0 403.5 jit_solution(14824272835183960789)
XLA Ops:
  7.2 1.4 copy-done
  8.6 6.3 %convolution_convert_fusion = bf16[1600,1600]{1,0:T(8,128)(2,1)} fusion(bf16[512,1600]{0,1:T(8,128)(2,1)S(1)} %copy-done, bf16[512,1600]{0,1:T(8,128)(2,1)} %param.12), kind=kOutput, calls=%fused_computation | convolution fusion | flops 2624000000 | bytes 8396800 | tf_op jit(solution)/shard_map/dot_general | solution.py:18
  15.0 1.4 copy-done.4
  16.7 48.7 %reduce-scatter.4.cloned.1.call-done = bf16[200,1600]{1,0:T(8,128)(2,1)} async-done(((bf16[1600,1600]{1,0:T(8,128)(2,1)}), bf16[200,1600]{1,0:T(8,128)(2,1)}) %reduce-scatter.4.cloned.1.call-update) | async-done | bytes 640016
  65.4 1.6 bitcast_add_fusion
  68.1 1.2 pad_maximum_fusion
  69.3 149.4 %all-reduce.3.cloned.1.call-done = f32[201,1600]{1,0:T(8,128)} async-done(((f32[201,1600]{1,0:T(8,128)}), f32[201,1600]{1,0:T(8,128)}) %all-reduce.3.cloned.1.call-update) | async-done | bytes 1286416 | tf_op jit(solution)/shard_map/psum | solution.py:27
  218.7 2.8 fusion.5
  221.8 25.7 %psum.22 = f32[2624]{0:T(1024)S(1)} all-reduce(f32[2624]{0:T(1024)S(1)} %pad_maximum_fusion.1), channel_id=1, replica_groups=mesh['grp'=32,'shard'=8] {'shard'}, use_global_device_ids=true, to_apply=%region_3.0 | all-reduce | flops 2624 | bytes 20992 | tf_op jit(solution)/shard_map/psum | solution.py:36
  247.7 2.9 cholesky.44
  251.9 2.4 custom-call.6
  254.6 1.7 convolution_bitcast_fusion.1
  256.4 24.8 %all-gather.10.cloned.1.call-done = f32[8,1600,32]{1,2,0:T(8,128)} async-done(((f32[1,1600,32]{1,2,0:T(8,128)}), f32[8,1600,32]{1,2,0:T(8,128)}) %all-gather.10.cloned.1.call-update) | async-done | bytes 1638416 | tf_op jit(solution)/shard_map/all_gather | solution.py:8
  281.2 1.6 reduce_sum.28
  282.7 1.4 fusion.2
  284.3 21.1 %psum.23 = f32[32,32]{0,1:T(8,128)S(1)} all-reduce(f32[32,32]{0,1:T(8,128)S(1)} %fusion.30), channel_id=1, replica_groups=mesh['grp'=32,'shard'=8] {'shard'}, use_global_device_ids=true, to_apply=%region_7.10 | all-reduce | flops 1024 | bytes 8192 | tf_op jit(solution)/shard_map/psum | solution.py:40
  305.4 2.9 cholesky.55
  309.7 2.4 custom-call.7
  312.4 1.7 convolution_bitcast_fusion
  314.1 29.4 %all-gather.12.cloned.1.call-done = f32[8,1600,32]{1,2,0:T(8,128)} async-done(((f32[1,1600,32]{1,2,0:T(8,128)}), f32[8,1600,32]{1,2,0:T(8,128)}) %all-gather.12.cloned.1.call-update) | async-done | bytes 1638416 | tf_op jit(solution)/shard_map/all_gather | solution.py:8
  343.5 1.6 reduce_sum.29
  345.0 4.7 %subtract_convert_fusion = (bf16[200,1600]{1,0:T(8,128)(2,1)}, f32[200,1600]{1,0:T(8,128)}, f32[1,200,1600]{2,1,0:T(8,128)}) fusion(bf16[200,1600]{1,0:T(8,128)(2,1)} %param.13, f32[200,1600]{1,0:T(8,128)} %param.15, f32[200,1600]{1,0:T(8,128)S(1)} %copy-done.3, f32[32,200]{1,0:T(8,128)S(1)} %fusion.12, f32[1600,32]{0,1:T(8,128)S(1)} %reduce_sum.29), kind=kOutput, calls=%fused_computation.9 | convolution fusion | flops 125171200 | bytes 6630400 | tf_op jit(solution)/shard_map/dot_general | solution.py:45
  350.4 39.2 %all-gather.8.cloned.1.call-done = bf16[1600,1600]{1,0:T(8,128)(2,1)} async-done(((bf16[200,1600]{1,0:T(8,128)(2,1)}), bf16[1600,1600]{1,0:T(8,128)(2,1)}) %all-gather.8.cloned.1.call-update) | async-done | bytes 5120016 | tf_op jit(solution)/shard_map/all_gather | solution.py:52
  389.6 7.4 %fusion = bf16[512,1600]{0,1:T(8,128)(2,1)} fusion(bf16[1600,1600]{1,0:T(8,128)(2,1)} %all-gather.8.cloned.1.call-done, bf16[512,1600]{0,1:T(8,128)(2,1)} %param.18), kind=kOutput, calls=%fused_computation.3 | convolution fusion | flops 2622259200 | bytes 8396800 | tf_op jit(solution)/shard_map/dot_general | solution.py:50
  (44 shorter events, 6.1 us)
Async XLA Ops:
  7.2 1.4 copy-start
  7.2 58.2 %reduce-scatter.4.cloned.1.call-start = ((), (), s32[]{:S(2)}) async-start(), calls=%async_computation.5 | async-start | bytes 5990400
  14.9 1.4 copy-start.4
  14.9 203.7 %all-reduce.3.cloned.1.call-start = ((), (), s32[]{:S(2)}) async-start(), calls=%async_computation.1 | async-start | bytes 2768896 | tf_op jit(solution)/shard_map/psum | solution.py:27
  67.0 1.1 copy-start.2
  68.1 150.6 %copy-start.5 = (f32[1600,32]{0,1:T(8,128)S(1)}, f32[1600,32]{0,1:T(8,128)}, u32[]{:S(2)}) copy-start(f32[1600,32]{0,1:T(8,128)} %param.17) | copy-start | bytes 614404
  69.3 211.9 %all-gather.10.cloned.1.call-start = ((), (), s32[]{:S(2)}) async-start(), calls=%async_computation.3 | async-start | bytes 1916928 | tf_op jit(solution)/shard_map/all_gather | solution.py:8
  218.7 3.0 copy-start.1
  256.3 87.1 %all-gather.12.cloned.1.call-start = ((), (), s32[]{:S(2)}) async-start(), calls=%async_computation.4 | async-start | bytes 1916928 | tf_op jit(solution)/shard_map/all_gather | solution.py:8
  314.0 31.0 %copy-start.3 = (f32[200,1600]{1,0:T(8,128)S(1)}, f32[200,1600]{1,0:T(8,128)}, u32[]{:S(2)}) copy-start(f32[200,1600]{1,0:T(8,128)} %copy-done.2) | copy-start | bytes 3840004
  314.1 75.5 %all-gather.8.cloned.1.call-start = ((), (), s32[]{:S(2)}) async-start(), calls=%async_computation.2 | async-start | bytes 5990400 | tf_op jit(solution)/shard_map/all_gather | solution.py:52
  345.0 4.8 %copy-start.6 = (f32[1600]{0:T(1024)S(1)}, f32[1600]{0:T(1024)}, u32[]{:S(2)}) copy-start(f32[1600]{0:T(1024)} %param.16) | copy-start | bytes 19204
Sparse Core Ops, SparseCore 0:
  15.1 50.2 reduce-scatter.3
  69.4 149.1 all-reduce.2
  256.4 24.6 all-gather.9
  314.2 29.2 all-gather.11
  349.9 39.5 all-gather.7
